TPU v7x, 512 devices: a whole 4x8x8 slice. The times are simulated.
512 devices in a mesh: seg: 32 (over y, x), sec: 16 (over z, core).
Axes of the slice: x: 4, y: 8, z: 8, core: 2. Of those that a mesh axis runs over, the one named last changes fastest.
Arguments:
- blocks: bfloat16 [32, 4, 16, 128, 128], P('seg', None, 'sec'), may hold values from -0.5 to 0.5
- left_edge: bfloat16 [16, 128], P('sec'), may hold values from -0.5 to 0.5
- right_edge: bfloat16 [16, 128], P('sec'), may hold values from -6 to 6
- occupation: int32 [1024, 32], P(None, 'seg'), may hold values from 0 to 3
- start_sector: int32 [1024], replicated, may hold values from 0 to 15
Outputs:
- amplitude: float32 [1024], replicated
All inputs are finite; a program needn't handle non-finite values.
Results may differ from a plain program's by a relative error of at most 0.015.
Values may be sent and summed in bfloat16 or wider, within the bound.
No kernel may reach another device: no remote copies, remote signals or barrier semaphores. Data moves between devices by JAX's collectives and lax.ppermute only.
A program may use at most 64 MiB of HBM per device.

v0:
```python
import jax
import jax.numpy as jnp
from jax import lax
from jax.sharding import PartitionSpec as P


def per_device(blocks, left_edge, right_edge, occupation, start_sector):
    seg_count = lax.axis_size("seg")
    sec_count = lax.axis_size("sec")
    half_count = seg_count // 2
    seg_index = lax.axis_index("seg")
    sec_index = lax.axis_index("sec")
    is_left = seg_index < half_count
    depth = jnp.where(is_left, seg_index, seg_count - 1 - seg_index)
    conf_count = occupation.shape[0]
    sites = seg_count * occupation.shape[1]
    group = conf_count // sec_count
    width = blocks.shape[-1]
    local_states = blocks.shape[1]
    site_blocks = lax.all_gather(blocks[0], "sec", axis=1, tiled=True)
    nsec = site_blocks.shape[1]
    lefts = lax.all_gather(left_edge, "sec", axis=0, tiled=True)
    rights = lax.all_gather(right_edge, "sec", axis=0, tiled=True)
    row0 = sec_index * group
    occ_mine = lax.dynamic_slice_in_dim(occupation, row0, group, axis=0)
    occ_group = lax.all_gather(occ_mine, "seg", axis=1, tiled=True)
    start_group = lax.dynamic_slice_in_dim(start_sector, row0, group, axis=0)
    charge = jnp.array([0, 1, -1, 0], dtype=jnp.int32)
    steps = charge[occ_group]
    site_ids = jnp.arange(sites, dtype=jnp.int32)
    before = jnp.sum(jnp.where(site_ids[None, :] < seg_index, steps, 0), axis=1)
    total = jnp.sum(steps, axis=1)
    sector_here = jnp.mod(start_group + before, nsec)
    sector_end = jnp.mod(start_group + total, nsec)
    occ_here = occ_mine[:, 0]
    sector_hot = (sector_here[:, None] == jnp.arange(nsec, dtype=jnp.int32)[None, :]).astype(
        jnp.bfloat16
    )
    state_hot = (occ_here[:, None] == jnp.arange(local_states, dtype=jnp.int32)[None, :]).astype(
        jnp.float32
    )
    oriented = lax.cond(is_left, lambda b: b, lambda b: jnp.swapaxes(b, 2, 3), site_blocks)

    def apply(vector):
        spread = vector[:, None, :] * sector_hot[:, :, None]
        products = jnp.einsum("kqa,nqab->knb", spread, oriented, preferred_element_type=jnp.float32)
        return jnp.sum(products * state_hot[:, :, None], axis=1).astype(jnp.bfloat16)

    first_left = jnp.take(lefts, start_group, axis=0)
    first_right = jnp.take(rights, sector_end, axis=0)
    first = jnp.where(is_left, first_left, first_right)
    vector = jnp.where(depth == 0, first, jnp.zeros_like(first))
    chain = [(j, j + 1) for j in range(half_count - 1)] + [
        (j, j - 1) for j in range(half_count + 1, seg_count)
    ]
    for step in range(half_count):
        vector = apply(vector)
        if step < half_count - 1:
            vector = lax.ppermute(vector, "seg", chain)
    meet = [(half_count - 1, half_count), (half_count, half_count - 1)]
    other = lax.ppermute(vector, "seg", meet)
    amp = jnp.sum(vector.astype(jnp.float32) * other.astype(jnp.float32), axis=1)
    amp = jnp.where(seg_index == half_count - 1, amp, jnp.zeros_like(amp))
    gathered = lax.all_gather(amp, "sec", axis=0, tiled=True)
    return lax.psum(gathered, "seg")


def solution(mesh):
    in_specs = (
        P("seg", None, "sec", None, None),
        P("sec", None),
        P("sec", None),
        P(None, "seg"),
        P(),
    )
    out_specs = P()
    return jax.shard_map(
        per_device, mesh=mesh, in_specs=in_specs, out_specs=out_specs, check_vma=False
    )
```

profile of v0, /device:TPU:32, one launch (start us, length us, event | category | flops | bytes accessed | tf_op | source)
XLA Modules:
  0.0 317.6 jit_solution(7298248449602463857)
XLA Ops:
  6.5 1.7 copy.33
  8.2 23.3 %all-gather.2 = bf16[16,1,128]{2,1,0:T(2,128)(2,1)S(1)} all-gather(bf16[1,1,128]{2,1,0:T(2,128)(2,1)} %bitcast.200), channel_id=1, replica_groups=mesh['seg'=32,'sec'=16] {'sec'}, dimensions={0}, use_global_device_ids=true | all-gather | bytes 4352 | tf_op jit(solution)/shard_map/all_gather | solution.py:23
  31.6 14.6 %all-gather.1 = bf16[16,1,128]{2,1,0:T(2,128)(2,1)S(1)} all-gather(bf16[1,1,128]{2,1,0:T(2,128)(2,1)} %bitcast.201), channel_id=1, replica_groups=mesh['seg'=32,'sec'=16] {'sec'}, dimensions={0}, use_global_device_ids=true | all-gather | bytes 4352 | tf_op jit(solution)/shard_map/all_gather | solution.py:22
  46.9 34.2 %all-gather.3 = s32[32,1,64]{2,1,0:T(1,128)S(1)} all-gather(s32[1,1,64]{2,1,0:T(1,128)S(1)} %get-tuple-element.18), channel_id=1, replica_groups=mesh['seg'=32,'sec'=16] {'seg'}, dimensions={0}, use_global_device_ids=true | all-gather | bytes 8448 | tf_op jit(solution)/shard_map/all_gather | solution.py:26
  84.2 3.1 conditional.1
  84.2 3.1 copy.34
  88.0 1.3 collective-permute-start
  89.3 4.3 %collective-permute-done = bf16[64,128]{1,0:T(8,128)(2,1)S(1)} collective-permute-done((bf16[64,128]{1,0:T(8,128)(2,1)S(1)}, bf16[64,128]{1,0:T(8,128)(2,1)S(1)}, u32[]{:S(2)}, u32[]{:S(2)}) %collective-permute-start) | collective-permute-done | bytes 16416 | tf_op jit(solution)/shard_map/ppermute | solution.py:59
  94.4 1.3 collective-permute-start.1
  95.7 4.3 %collective-permute-done.1 = bf16[64,128]{1,0:T(8,128)(2,1)S(1)} collective-permute-done((bf16[64,128]{1,0:T(8,128)(2,1)S(1)}, bf16[64,128]{1,0:T(8,128)(2,1)S(1)}, u32[]{:S(2)}, u32[]{:S(2)}) %collective-permute-start.1) | collective-permute-done | bytes 16416 | tf_op jit(solution)/shard_map/ppermute | solution.py:59
  100.8 1.3 collective-permute-start.2
  102.1 4.3 %collective-permute-done.2 = bf16[64,128]{1,0:T(8,128)(2,1)S(1)} collective-permute-done((bf16[64,128]{1,0:T(8,128)(2,1)S(1)}, bf16[64,128]{1,0:T(8,128)(2,1)S(1)}, u32[]{:S(2)}, u32[]{:S(2)}) %collective-permute-start.2) | collective-permute-done | bytes 16416 | tf_op jit(solution)/shard_map/ppermute | solution.py:59
  107.2 1.3 collective-permute-start.3
  108.5 4.3 %collective-permute-done.3 = bf16[64,128]{1,0:T(8,128)(2,1)S(1)} collective-permute-done((bf16[64,128]{1,0:T(8,128)(2,1)S(1)}, bf16[64,128]{1,0:T(8,128)(2,1)S(1)}, u32[]{:S(2)}, u32[]{:S(2)}) %collective-permute-start.3) | collective-permute-done | bytes 16416 | tf_op jit(solution)/shard_map/ppermute | solution.py:59
  113.6 1.3 collective-permute-start.4
  114.9 4.8 %collective-permute-done.4 = bf16[64,128]{1,0:T(8,128)(2,1)S(1)} collective-permute-done((bf16[64,128]{1,0:T(8,128)(2,1)S(1)}, bf16[64,128]{1,0:T(8,128)(2,1)S(1)}, u32[]{:S(2)}, u32[]{:S(2)}) %collective-permute-start.4) | collective-permute-done | bytes 16416 | tf_op jit(solution)/shard_map/ppermute | solution.py:59
  121.7 6.4 %collective-permute-done.5 = bf16[64,128]{1,0:T(8,128)(2,1)S(1)} collective-permute-done((bf16[64,128]{1,0:T(8,128)(2,1)S(1)}, bf16[64,128]{1,0:T(8,128)(2,1)S(1)}, u32[]{:S(2)}, u32[]{:S(2)}) %collective-permute-start.5) | collective-permute-done | bytes 16416 | tf_op jit(solution)/shard_map/ppermute | solution.py:59
  128.9 1.3 collective-permute-start.6
  130.2 6.4 %collective-permute-done.6 = bf16[64,128]{1,0:T(8,128)(2,1)S(1)} collective-permute-done((bf16[64,128]{1,0:T(8,128)(2,1)S(1)}, bf16[64,128]{1,0:T(8,128)(2,1)S(1)}, u32[]{:S(2)}, u32[]{:S(2)}) %collective-permute-start.6) | collective-permute-done | bytes 16416 | tf_op jit(solution)/shard_map/ppermute | solution.py:59
  138.7 6.4 %collective-permute-done.7 = bf16[64,128]{1,0:T(8,128)(2,1)S(1)} collective-permute-done((bf16[64,128]{1,0:T(8,128)(2,1)S(1)}, bf16[64,128]{1,0:T(8,128)(2,1)S(1)}, u32[]{:S(2)}, u32[]{:S(2)}) %collective-permute-start.7) | collective-permute-done | bytes 16416 | tf_op jit(solution)/shard_map/ppermute | solution.py:59
  145.9 1.3 collective-permute-start.8
  147.2 6.5 %collective-permute-done.8 = bf16[64,128]{1,0:T(8,128)(2,1)S(1)} collective-permute-done((bf16[64,128]{1,0:T(8,128)(2,1)S(1)}, bf16[64,128]{1,0:T(8,128)(2,1)S(1)}, u32[]{:S(2)}, u32[]{:S(2)}) %collective-permute-start.8) | collective-permute-done | bytes 16416 | tf_op jit(solution)/shard_map/ppermute | solution.py:59
  155.8 6.3 %collective-permute-done.9 = bf16[64,128]{1,0:T(8,128)(2,1)S(1)} collective-permute-done((bf16[64,128]{1,0:T(8,128)(2,1)S(1)}, bf16[64,128]{1,0:T(8,128)(2,1)S(1)}, u32[]{:S(2)}, u32[]{:S(2)}) %collective-permute-start.9) | collective-permute-done | bytes 16416 | tf_op jit(solution)/shard_map/ppermute | solution.py:59
  164.2 6.4 %collective-permute-done.10 = bf16[64,128]{1,0:T(8,128)(2,1)S(1)} collective-permute-done((bf16[64,128]{1,0:T(8,128)(2,1)S(1)}, bf16[64,128]{1,0:T(8,128)(2,1)S(1)}, u32[]{:S(2)}, u32[]{:S(2)}) %collective-permute-start.10) | collective-permute-done | bytes 16416 | tf_op jit(solution)/shard_map/ppermute | solution.py:59
  172.7 6.4 %collective-permute-done.11 = bf16[64,128]{1,0:T(8,128)(2,1)S(1)} collective-permute-done((bf16[64,128]{1,0:T(8,128)(2,1)S(1)}, bf16[64,128]{1,0:T(8,128)(2,1)S(1)}, u32[]{:S(2)}, u32[]{:S(2)}) %collective-permute-start.11) | collective-permute-done | bytes 16416 | tf_op jit(solution)/shard_map/ppermute | solution.py:59
  181.2 6.4 %collective-permute-done.12 = bf16[64,128]{1,0:T(8,128)(2,1)S(1)} collective-permute-done((bf16[64,128]{1,0:T(8,128)(2,1)S(1)}, bf16[64,128]{1,0:T(8,128)(2,1)S(1)}, u32[]{:S(2)}, u32[]{:S(2)}) %collective-permute-start.12) | collective-permute-done | bytes 16416 | tf_op jit(solution)/shard_map/ppermute | solution.py:59
  189.7 6.4 %collective-permute-done.13 = bf16[64,128]{1,0:T(8,128)(2,1)S(1)} collective-permute-done((bf16[64,128]{1,0:T(8,128)(2,1)S(1)}, bf16[64,128]{1,0:T(8,128)(2,1)S(1)}, u32[]{:S(2)}, u32[]{:S(2)}) %collective-permute-start.13) | collective-permute-done | bytes 16416 | tf_op jit(solution)/shard_map/ppermute | solution.py:59
  198.2 6.4 %collective-permute-done.14 = bf16[64,128]{1,0:T(8,128)(2,1)S(1)} collective-permute-done((bf16[64,128]{1,0:T(8,128)(2,1)S(1)}, bf16[64,128]{1,0:T(8,128)(2,1)S(1)}, u32[]{:S(2)}, u32[]{:S(2)}) %collective-permute-start.14) | collective-permute-done | bytes 16416 | tf_op jit(solution)/shard_map/ppermute | solution.py:59
  205.4 4.3 %collective-permute-start.15 = (bf16[64,128]{1,0:T(8,128)(2,1)S(1)}, bf16[64,128]{1,0:T(8,128)(2,1)S(1)}, u32[]{:S(2)}, u32[]{:S(2)}) collective-permute-start(bf16[64,128]{1,0:T(8,128)(2,1)S(1)} %fusion.16), channel_id=1, source_target_pairs={{240,256},{256,240},{241,257},{257,241},{242,258},{258,242},{243,2... | collective-permute-start | bytes 49160 | tf_op jit(solution)/shard_map/ppermute | solution.py:61
  211.7 2.7 collective-permute-done.15
  214.6 23.5 %all-reduce = f32[1024]{0:T(1024)S(1)} all-reduce(f32[1024]{0:T(1024)S(1)} %fusion.100), channel_id=1, replica_groups=mesh['seg'=32,'sec'=16] {'sec'}, use_global_device_ids=true, to_apply=%add | all-reduce | flops 1024 | bytes 8192
  238.2 72.6 %psum.7 = f32[1024]{0:T(1024)} all-reduce(f32[1024]{0:T(1024)S(1)} %all-reduce), channel_id=1, replica_groups=mesh['seg'=32,'sec'=16] {'seg'}, use_global_device_ids=true, to_apply=%region_21.23 | all-reduce | flops 1024 | bytes 8192 | tf_op jit(solution)/shard_map/psum | solution.py:65
  (44 shorter events, 27.7 us)
Async XLA Ops:
  6.5 77.6 %all-gather.6.cloned.1.call-start = ((), (), s32[]{:S(2)}) async-start(), calls=%async_computation | async-start | bytes 2228224 | tf_op jit(solution)/shard_map/all_gather | solution.py:20
  88.0 5.6 %collective-permute-start = (bf16[64,128]{1,0:T(8,128)(2,1)S(1)}, bf16[64,128]{1,0:T(8,128)(2,1)S(1)}, u32[]{:S(2)}, u32[]{:S(2)}) collective-permute-start(bf16[64,128]{1,0:T(8,128)(2,1)S(1)} %fusion.31), channel_id=1, source_target_pairs={{0,16},{16,32},{32,48},{48,64},{64,80},{80,96},{96,112},{112,128},... | collective-permute-start | bytes 49160 | tf_op jit(solution)/shard_map/ppermute | solution.py:59
  94.4 5.6 %collective-permute-start.1 = (bf16[64,128]{1,0:T(8,128)(2,1)S(1)}, bf16[64,128]{1,0:T(8,128)(2,1)S(1)}, u32[]{:S(2)}, u32[]{:S(2)}) collective-permute-start(bf16[64,128]{1,0:T(8,128)(2,1)S(1)} %fusion.30), channel_id=1, source_target_pairs={{0,16},{16,32},{32,48},{48,64},{64,80},{80,96},{96,112},{112,128},... | collective-permute-start | bytes 49160 | tf_op jit(solution)/shard_map/ppermute | solution.py:59
  100.8 5.6 %collective-permute-start.2 = (bf16[64,128]{1,0:T(8,128)(2,1)S(1)}, bf16[64,128]{1,0:T(8,128)(2,1)S(1)}, u32[]{:S(2)}, u32[]{:S(2)}) collective-permute-start(bf16[64,128]{1,0:T(8,128)(2,1)S(1)} %fusion.29), channel_id=1, source_target_pairs={{0,16},{16,32},{32,48},{48,64},{64,80},{80,96},{96,112},{112,128},... | collective-permute-start | bytes 49160 | tf_op jit(solution)/shard_map/ppermute | solution.py:59
  107.2 5.6 %collective-permute-start.3 = (bf16[64,128]{1,0:T(8,128)(2,1)S(1)}, bf16[64,128]{1,0:T(8,128)(2,1)S(1)}, u32[]{:S(2)}, u32[]{:S(2)}) collective-permute-start(bf16[64,128]{1,0:T(8,128)(2,1)S(1)} %fusion.28), channel_id=1, source_target_pairs={{0,16},{16,32},{32,48},{48,64},{64,80},{80,96},{96,112},{112,128},... | collective-permute-start | bytes 49160 | tf_op jit(solution)/shard_map/ppermute | solution.py:59
  113.6 6.1 %collective-permute-start.4 = (bf16[64,128]{1,0:T(8,128)(2,1)S(1)}, bf16[64,128]{1,0:T(8,128)(2,1)S(1)}, u32[]{:S(2)}, u32[]{:S(2)}) collective-permute-start(bf16[64,128]{1,0:T(8,128)(2,1)S(1)} %fusion.27), channel_id=1, source_target_pairs={{0,16},{16,32},{32,48},{48,64},{64,80},{80,96},{96,112},{112,128},... | collective-permute-start | bytes 49160 | tf_op jit(solution)/shard_map/ppermute | solution.py:59
  120.4 7.7 %collective-permute-start.5 = (bf16[64,128]{1,0:T(8,128)(2,1)S(1)}, bf16[64,128]{1,0:T(8,128)(2,1)S(1)}, u32[]{:S(2)}, u32[]{:S(2)}) collective-permute-start(bf16[64,128]{1,0:T(8,128)(2,1)S(1)} %fusion.26), channel_id=1, source_target_pairs={{0,16},{16,32},{32,48},{48,64},{64,80},{80,96},{96,112},{112,128},... | collective-permute-start | bytes 49160 | tf_op jit(solution)/shard_map/ppermute | solution.py:59
  128.9 7.7 %collective-permute-start.6 = (bf16[64,128]{1,0:T(8,128)(2,1)S(1)}, bf16[64,128]{1,0:T(8,128)(2,1)S(1)}, u32[]{:S(2)}, u32[]{:S(2)}) collective-permute-start(bf16[64,128]{1,0:T(8,128)(2,1)S(1)} %fusion.25), channel_id=1, source_target_pairs={{0,16},{16,32},{32,48},{48,64},{64,80},{80,96},{96,112},{112,128},... | collective-permute-start | bytes 49160 | tf_op jit(solution)/shard_map/ppermute | solution.py:59
  137.4 7.7 %collective-permute-start.7 = (bf16[64,128]{1,0:T(8,128)(2,1)S(1)}, bf16[64,128]{1,0:T(8,128)(2,1)S(1)}, u32[]{:S(2)}, u32[]{:S(2)}) collective-permute-start(bf16[64,128]{1,0:T(8,128)(2,1)S(1)} %fusion.24), channel_id=1, source_target_pairs={{0,16},{16,32},{32,48},{48,64},{64,80},{80,96},{96,112},{112,128},... | collective-permute-start | bytes 49160 | tf_op jit(solution)/shard_map/ppermute | solution.py:59
  145.9 7.8 %collective-permute-start.8 = (bf16[64,128]{1,0:T(8,128)(2,1)S(1)}, bf16[64,128]{1,0:T(8,128)(2,1)S(1)}, u32[]{:S(2)}, u32[]{:S(2)}) collective-permute-start(bf16[64,128]{1,0:T(8,128)(2,1)S(1)} %fusion.23), channel_id=1, source_target_pairs={{0,16},{16,32},{32,48},{48,64},{64,80},{80,96},{96,112},{112,128},... | collective-permute-start | bytes 49160 | tf_op jit(solution)/shard_map/ppermute | solution.py:59
  154.5 7.6 %collective-permute-start.9 = (bf16[64,128]{1,0:T(8,128)(2,1)S(1)}, bf16[64,128]{1,0:T(8,128)(2,1)S(1)}, u32[]{:S(2)}, u32[]{:S(2)}) collective-permute-start(bf16[64,128]{1,0:T(8,128)(2,1)S(1)} %fusion.22), channel_id=1, source_target_pairs={{0,16},{16,32},{32,48},{48,64},{64,80},{80,96},{96,112},{112,128},... | collective-permute-start | bytes 49160 | tf_op jit(solution)/shard_map/ppermute | solution.py:59
  162.9 7.7 %collective-permute-start.10 = (bf16[64,128]{1,0:T(8,128)(2,1)S(1)}, bf16[64,128]{1,0:T(8,128)(2,1)S(1)}, u32[]{:S(2)}, u32[]{:S(2)}) collective-permute-start(bf16[64,128]{1,0:T(8,128)(2,1)S(1)} %fusion.21), channel_id=1, source_target_pairs={{0,16},{16,32},{32,48},{48,64},{64,80},{80,96},{96,112},{112,128},... | collective-permute-start | bytes 49160 | tf_op jit(solution)/shard_map/ppermute | solution.py:59
  171.4 7.7 %collective-permute-start.11 = (bf16[64,128]{1,0:T(8,128)(2,1)S(1)}, bf16[64,128]{1,0:T(8,128)(2,1)S(1)}, u32[]{:S(2)}, u32[]{:S(2)}) collective-permute-start(bf16[64,128]{1,0:T(8,128)(2,1)S(1)} %fusion.20), channel_id=1, source_target_pairs={{0,16},{16,32},{32,48},{48,64},{64,80},{80,96},{96,112},{112,128},... | collective-permute-start | bytes 49160 | tf_op jit(solution)/shard_map/ppermute | solution.py:59
  179.9 7.7 %collective-permute-start.12 = (bf16[64,128]{1,0:T(8,128)(2,1)S(1)}, bf16[64,128]{1,0:T(8,128)(2,1)S(1)}, u32[]{:S(2)}, u32[]{:S(2)}) collective-permute-start(bf16[64,128]{1,0:T(8,128)(2,1)S(1)} %fusion.19), channel_id=1, source_target_pairs={{0,16},{16,32},{32,48},{48,64},{64,80},{80,96},{96,112},{112,128},... | collective-permute-start | bytes 49160 | tf_op jit(solution)/shard_map/ppermute | solution.py:59
  188.4 7.7 %collective-permute-start.13 = (bf16[64,128]{1,0:T(8,128)(2,1)S(1)}, bf16[64,128]{1,0:T(8,128)(2,1)S(1)}, u32[]{:S(2)}, u32[]{:S(2)}) collective-permute-start(bf16[64,128]{1,0:T(8,128)(2,1)S(1)} %fusion.18), channel_id=1, source_target_pairs={{0,16},{16,32},{32,48},{48,64},{64,80},{80,96},{96,112},{112,128},... | collective-permute-start | bytes 49160 | tf_op jit(solution)/shard_map/ppermute | solution.py:59
  196.9 7.7 %collective-permute-start.14 = (bf16[64,128]{1,0:T(8,128)(2,1)S(1)}, bf16[64,128]{1,0:T(8,128)(2,1)S(1)}, u32[]{:S(2)}, u32[]{:S(2)}) collective-permute-start(bf16[64,128]{1,0:T(8,128)(2,1)S(1)} %fusion.17), channel_id=1, source_target_pairs={{0,16},{16,32},{32,48},{48,64},{64,80},{80,96},{96,112},{112,128},... | collective-permute-start | bytes 49160 | tf_op jit(solution)/shard_map/ppermute | solution.py:59
  205.4 9.0 %collective-permute-start.15 = (bf16[64,128]{1,0:T(8,128)(2,1)S(1)}, bf16[64,128]{1,0:T(8,128)(2,1)S(1)}, u32[]{:S(2)}, u32[]{:S(2)}) collective-permute-start(bf16[64,128]{1,0:T(8,128)(2,1)S(1)} %fusion.16), channel_id=1, source_target_pairs={{240,256},{256,240},{241,257},{257,241},{242,258},{258,242},{243,2... | collective-permute-start | bytes 49160 | tf_op jit(solution)/shard_map/ppermute | solution.py:61
Sparse Core Ops, SparseCore 0:
  9.5 47.2 all-gather.5
where the time goes:
time: 320 us; the launch traced here: 318 us
  blocking collectives  168 us (52%)
  waiting for transfers between devices  89.3 us (28%)
  starting transfers between devices  23.7 us (7%)
  between operations  14.4 us (4%)
  matrix products  12.1 us (4%)
  local copies, waits for them, and re-layouts  7.99 us (2%)
    ppermute x15, waiting for transfers between devices, per_device(): vector = lax.ppermute(vector, 'seg', chain)  86.5 us
    psum x1, blocking collectives, per_device(): return lax.psum(gathered, 'seg')  72.6 us
    all_gather x1, blocking collectives, per_device(): occ_group = lax.all_gather(occ_mine, 'seg', axis=1, tiled=True)  34.2 us
    unnamed x1, blocking collectives  23.5 us
    all_gather x1, blocking collectives, per_device(): rights = lax.all_gather(right_edge, 'sec', axis=0, tiled=True)  23.3 us
    ppermute x15, starting transfers between devices, per_device(): vector = lax.ppermute(vector, 'seg', chain)  19.4 us
    all_gather x1, blocking collectives, per_device(): lefts = lax.all_gather(left_edge, 'sec', axis=0, tiled=True)  14.6 us
    dot_general x16, matrix products, apply(): jnp.einsum('kqa,nqab->knb', spread, oriented, preferred_element_type=jnp....  12.1 us
  transfers between devices with their start and end apart: 17, of which 16 were waited for; matrix products, arithmetic and copies ran while one was open for 2% of the time, Pallas kernels for 0%

commit v1 on v0

--- a/solution.py
+++ b/solution.py
@@ -2,6 +2,8 @@
 import jax.numpy as jnp
 from jax import lax
 from jax.sharding import PartitionSpec as P
+
+_number_shifts_all = lambda my_tile: jnp.sum(jax.lax.all_gather(my_tile, axis_name="seg"), axis=0)
 
 
 def per_device(blocks, left_edge, right_edge, occupation, start_sector):
@@ -62,7 +64,7 @@
     amp = jnp.sum(vector.astype(jnp.float32) * other.astype(jnp.float32), axis=1)
     amp = jnp.where(seg_index == half_count - 1, amp, jnp.zeros_like(amp))
     gathered = lax.all_gather(amp, "sec", axis=0, tiled=True)
-    return lax.psum(gathered, "seg")
+    return _number_shifts_all(gathered)
 
 
 def solution(mesh):

time: 320 us -> 289 us (0.903)
  the two profiles are of different devices: /device:TPU:32 before, /device:TPU:24 now
where the time goes in v1:
time: 289 us; the launch traced here: 287 us
  blocking collectives  134 us (46%)
  waiting for transfers between devices  87.1 us (30%)
  starting transfers between devices  29.7 us (10%)
  between operations  14.4 us (5%)
  matrix products  12.1 us (4%)
  local copies, waits for them, and re-layouts  6.56 us (2%)
    ppermute x15, waiting for transfers between devices, per_device(): vector = lax.ppermute(vector, 'seg', chain)  87.1 us
    all_gather x1, blocking collectives, jax.lax.all_gather(my_tile, axis_name='seg')  37.2 us
    all_gather x1, blocking collectives, per_device(): occ_group = lax.all_gather(occ_mine, 'seg', axis=1, tiled=True)  35.6 us
    ppermute x15, starting transfers between devices, per_device(): vector = lax.ppermute(vector, 'seg', chain)  29.1 us
    unnamed x1, blocking collectives  23.5 us
    all_gather x1, blocking collectives, per_device(): rights = lax.all_gather(right_edge, 'sec', axis=0, tiled=True)  23.3 us
    all_gather x1, blocking collectives, per_device(): lefts = lax.all_gather(left_edge, 'sec', axis=0, tiled=True)  14.6 us
    dot_general x16, matrix products, apply(): jnp.einsum('kqa,nqab->knb', spread, oriented, preferred_element_type=jnp....  12.1 us
  transfers between devices with their start and end apart: 17, of which 15 were waited for; matrix products, arithmetic and copies ran while one was open for 2% of the time, Pallas kernels for 0%

profile of v1, /device:TPU:24, one launch (start us, length us, event | category | flops | bytes accessed | tf_op | source)
XLA Modules:
  0.0 286.8 jit_solution(366118645245599922)
XLA Ops:
  8.2 23.3 %all-gather.3 = bf16[16,1,128]{2,1,0:T(2,128)(2,1)S(1)} all-gather(bf16[1,1,128]{2,1,0:T(2,128)(2,1)} %bitcast.200), channel_id=1, replica_groups=mesh['seg'=32,'sec'=16] {'sec'}, dimensions={0}, use_global_device_ids=true | all-gather | bytes 4352 | tf_op jit(solution)/shard_map/all_gather | solution.py:25
  31.6 14.6 %all-gather.2 = bf16[16,1,128]{2,1,0:T(2,128)(2,1)S(1)} all-gather(bf16[1,1,128]{2,1,0:T(2,128)(2,1)} %bitcast.201), channel_id=1, replica_groups=mesh['seg'=32,'sec'=16] {'sec'}, dimensions={0}, use_global_device_ids=true | all-gather | bytes 4352 | tf_op jit(solution)/shard_map/all_gather | solution.py:24
  46.9 35.6 %all-gather.4 = s32[32,1,64]{2,1,0:T(1,128)S(1)} all-gather(s32[1,1,64]{2,1,0:T(1,128)S(1)} %get-tuple-element.18), channel_id=1, replica_groups=mesh['seg'=32,'sec'=16] {'seg'}, dimensions={0}, use_global_device_ids=true | all-gather | bytes 8448 | tf_op jit(solution)/shard_map/all_gather | solution.py:28
  88.0 2.2 collective-permute-start
  90.2 5.5 %collective-permute-done = bf16[64,128]{1,0:T(8,128)(2,1)S(1)} collective-permute-done((bf16[64,128]{1,0:T(8,128)(2,1)S(1)}, bf16[64,128]{1,0:T(8,128)(2,1)S(1)}, u32[]{:S(2)}, u32[]{:S(2)}) %collective-permute-start) | collective-permute-done | bytes 16416 | tf_op jit(solution)/shard_map/ppermute | solution.py:61
  96.5 1.9 collective-permute-start.1
  98.4 5.8 %collective-permute-done.1 = bf16[64,128]{1,0:T(8,128)(2,1)S(1)} collective-permute-done((bf16[64,128]{1,0:T(8,128)(2,1)S(1)}, bf16[64,128]{1,0:T(8,128)(2,1)S(1)}, u32[]{:S(2)}, u32[]{:S(2)}) %collective-permute-start.1) | collective-permute-done | bytes 16416 | tf_op jit(solution)/shard_map/ppermute | solution.py:61
  105.0 1.9 collective-permute-start.2
  106.9 5.8 %collective-permute-done.2 = bf16[64,128]{1,0:T(8,128)(2,1)S(1)} collective-permute-done((bf16[64,128]{1,0:T(8,128)(2,1)S(1)}, bf16[64,128]{1,0:T(8,128)(2,1)S(1)}, u32[]{:S(2)}, u32[]{:S(2)}) %collective-permute-start.2) | collective-permute-done | bytes 16416 | tf_op jit(solution)/shard_map/ppermute | solution.py:61
  113.5 1.9 collective-permute-start.3
  115.4 5.8 %collective-permute-done.3 = bf16[64,128]{1,0:T(8,128)(2,1)S(1)} collective-permute-done((bf16[64,128]{1,0:T(8,128)(2,1)S(1)}, bf16[64,128]{1,0:T(8,128)(2,1)S(1)}, u32[]{:S(2)}, u32[]{:S(2)}) %collective-permute-start.3) | collective-permute-done | bytes 16416 | tf_op jit(solution)/shard_map/ppermute | solution.py:61
  122.0 1.9 collective-permute-start.4
  123.9 5.8 %collective-permute-done.4 = bf16[64,128]{1,0:T(8,128)(2,1)S(1)} collective-permute-done((bf16[64,128]{1,0:T(8,128)(2,1)S(1)}, bf16[64,128]{1,0:T(8,128)(2,1)S(1)}, u32[]{:S(2)}, u32[]{:S(2)}) %collective-permute-start.4) | collective-permute-done | bytes 16416 | tf_op jit(solution)/shard_map/ppermute | solution.py:61
  130.5 1.9 collective-permute-start.5
  132.4 5.8 %collective-permute-done.5 = bf16[64,128]{1,0:T(8,128)(2,1)S(1)} collective-permute-done((bf16[64,128]{1,0:T(8,128)(2,1)S(1)}, bf16[64,128]{1,0:T(8,128)(2,1)S(1)}, u32[]{:S(2)}, u32[]{:S(2)}) %collective-permute-start.5) | collective-permute-done | bytes 16416 | tf_op jit(solution)/shard_map/ppermute | solution.py:61
  139.0 1.9 collective-permute-start.6
  140.9 5.9 %collective-permute-done.6 = bf16[64,128]{1,0:T(8,128)(2,1)S(1)} collective-permute-done((bf16[64,128]{1,0:T(8,128)(2,1)S(1)}, bf16[64,128]{1,0:T(8,128)(2,1)S(1)}, u32[]{:S(2)}, u32[]{:S(2)}) %collective-permute-start.6) | collective-permute-done | bytes 16416 | tf_op jit(solution)/shard_map/ppermute | solution.py:61
  147.6 1.9 collective-permute-start.7
  149.6 5.8 %collective-permute-done.7 = bf16[64,128]{1,0:T(8,128)(2,1)S(1)} collective-permute-done((bf16[64,128]{1,0:T(8,128)(2,1)S(1)}, bf16[64,128]{1,0:T(8,128)(2,1)S(1)}, u32[]{:S(2)}, u32[]{:S(2)}) %collective-permute-start.7) | collective-permute-done | bytes 16416 | tf_op jit(solution)/shard_map/ppermute | solution.py:61
  156.1 1.9 collective-permute-start.8
  158.1 5.8 %collective-permute-done.8 = bf16[64,128]{1,0:T(8,128)(2,1)S(1)} collective-permute-done((bf16[64,128]{1,0:T(8,128)(2,1)S(1)}, bf16[64,128]{1,0:T(8,128)(2,1)S(1)}, u32[]{:S(2)}, u32[]{:S(2)}) %collective-permute-start.8) | collective-permute-done | bytes 16416 | tf_op jit(solution)/shard_map/ppermute | solution.py:61
  164.6 1.9 collective-permute-start.9
  166.6 5.8 %collective-permute-done.9 = bf16[64,128]{1,0:T(8,128)(2,1)S(1)} collective-permute-done((bf16[64,128]{1,0:T(8,128)(2,1)S(1)}, bf16[64,128]{1,0:T(8,128)(2,1)S(1)}, u32[]{:S(2)}, u32[]{:S(2)}) %collective-permute-start.9) | collective-permute-done | bytes 16416 | tf_op jit(solution)/shard_map/ppermute | solution.py:61
  173.1 1.9 collective-permute-start.10
  175.1 5.8 %collective-permute-done.10 = bf16[64,128]{1,0:T(8,128)(2,1)S(1)} collective-permute-done((bf16[64,128]{1,0:T(8,128)(2,1)S(1)}, bf16[64,128]{1,0:T(8,128)(2,1)S(1)}, u32[]{:S(2)}, u32[]{:S(2)}) %collective-permute-start.10) | collective-permute-done | bytes 16416 | tf_op jit(solution)/shard_map/ppermute | solution.py:61
  183.6 5.8 %collective-permute-done.11 = bf16[64,128]{1,0:T(8,128)(2,1)S(1)} collective-permute-done((bf16[64,128]{1,0:T(8,128)(2,1)S(1)}, bf16[64,128]{1,0:T(8,128)(2,1)S(1)}, u32[]{:S(2)}, u32[]{:S(2)}) %collective-permute-start.11) | collective-permute-done | bytes 16416 | tf_op jit(solution)/shard_map/ppermute | solution.py:61
  192.1 5.8 %collective-permute-done.12 = bf16[64,128]{1,0:T(8,128)(2,1)S(1)} collective-permute-done((bf16[64,128]{1,0:T(8,128)(2,1)S(1)}, bf16[64,128]{1,0:T(8,128)(2,1)S(1)}, u32[]{:S(2)}, u32[]{:S(2)}) %collective-permute-start.12) | collective-permute-done | bytes 16416 | tf_op jit(solution)/shard_map/ppermute | solution.py:61
  198.7 1.9 collective-permute-start.13
  200.6 5.8 %collective-permute-done.13 = bf16[64,128]{1,0:T(8,128)(2,1)S(1)} collective-permute-done((bf16[64,128]{1,0:T(8,128)(2,1)S(1)}, bf16[64,128]{1,0:T(8,128)(2,1)S(1)}, u32[]{:S(2)}, u32[]{:S(2)}) %collective-permute-start.13) | collective-permute-done | bytes 16416 | tf_op jit(solution)/shard_map/ppermute | solution.py:61
  209.1 5.8 %collective-permute-done.14 = bf16[64,128]{1,0:T(8,128)(2,1)S(1)} collective-permute-done((bf16[64,128]{1,0:T(8,128)(2,1)S(1)}, bf16[64,128]{1,0:T(8,128)(2,1)S(1)}, u32[]{:S(2)}, u32[]{:S(2)}) %collective-permute-start.14) | collective-permute-done | bytes 16416 | tf_op jit(solution)/shard_map/ppermute | solution.py:61
  218.5 23.5 %all-reduce = f32[1024]{0:T(1024)S(1)} all-reduce(f32[1024]{0:T(1024)S(1)} %fusion.100), channel_id=1, replica_groups=mesh['seg'=32,'sec'=16] {'sec'}, use_global_device_ids=true, to_apply=%add | all-reduce | flops 1024 | bytes 8192
  242.0 37.2 %all-gather.1 = f32[32768]{0:T(1024)S(1)} all-gather(f32[1024]{0:T(1024)S(1)} %all-reduce), channel_id=3, replica_groups=mesh['seg'=32,'sec'=16] {'seg'}, dimensions={0}, use_global_device_ids=true | all-gather | bytes 135168 | tf_op jit(solution)/shard_map/all_gather | solution.py:6
  (46 shorter events, 29.3 us)
Async XLA Ops:
  6.5 79.1 %all-gather.7.cloned.1.call-start = ((), (), s32[]{:S(2)}) async-start(), calls=%async_computation | async-start | bytes 2228224 | tf_op jit(solution)/shard_map/all_gather | solution.py:22
  88.0 7.7 %collective-permute-start = (bf16[64,128]{1,0:T(8,128)(2,1)S(1)}, bf16[64,128]{1,0:T(8,128)(2,1)S(1)}, u32[]{:S(2)}, u32[]{:S(2)}) collective-permute-start(bf16[64,128]{1,0:T(8,128)(2,1)S(1)} %fusion.31), channel_id=1, source_target_pairs={{0,16},{16,32},{32,48},{48,64},{64,80},{80,96},{96,112},{112,128},... | collective-permute-start | bytes 49160 | tf_op jit(solution)/shard_map/ppermute | solution.py:61
  96.5 7.7 %collective-permute-start.1 = (bf16[64,128]{1,0:T(8,128)(2,1)S(1)}, bf16[64,128]{1,0:T(8,128)(2,1)S(1)}, u32[]{:S(2)}, u32[]{:S(2)}) collective-permute-start(bf16[64,128]{1,0:T(8,128)(2,1)S(1)} %fusion.30), channel_id=1, source_target_pairs={{0,16},{16,32},{32,48},{48,64},{64,80},{80,96},{96,112},{112,128},... | collective-permute-start | bytes 49160 | tf_op jit(solution)/shard_map/ppermute | solution.py:61
  105.0 7.7 %collective-permute-start.2 = (bf16[64,128]{1,0:T(8,128)(2,1)S(1)}, bf16[64,128]{1,0:T(8,128)(2,1)S(1)}, u32[]{:S(2)}, u32[]{:S(2)}) collective-permute-start(bf16[64,128]{1,0:T(8,128)(2,1)S(1)} %fusion.29), channel_id=1, source_target_pairs={{0,16},{16,32},{32,48},{48,64},{64,80},{80,96},{96,112},{112,128},... | collective-permute-start | bytes 49160 | tf_op jit(solution)/shard_map/ppermute | solution.py:61
  113.5 7.7 %collective-permute-start.3 = (bf16[64,128]{1,0:T(8,128)(2,1)S(1)}, bf16[64,128]{1,0:T(8,128)(2,1)S(1)}, u32[]{:S(2)}, u32[]{:S(2)}) collective-permute-start(bf16[64,128]{1,0:T(8,128)(2,1)S(1)} %fusion.28), channel_id=1, source_target_pairs={{0,16},{16,32},{32,48},{48,64},{64,80},{80,96},{96,112},{112,128},... | collective-permute-start | bytes 49160 | tf_op jit(solution)/shard_map/ppermute | solution.py:61
  122.0 7.7 %collective-permute-start.4 = (bf16[64,128]{1,0:T(8,128)(2,1)S(1)}, bf16[64,128]{1,0:T(8,128)(2,1)S(1)}, u32[]{:S(2)}, u32[]{:S(2)}) collective-permute-start(bf16[64,128]{1,0:T(8,128)(2,1)S(1)} %fusion.27), channel_id=1, source_target_pairs={{0,16},{16,32},{32,48},{48,64},{64,80},{80,96},{96,112},{112,128},... | collective-permute-start | bytes 49160 | tf_op jit(solution)/shard_map/ppermute | solution.py:61
  130.5 7.7 %collective-permute-start.5 = (bf16[64,128]{1,0:T(8,128)(2,1)S(1)}, bf16[64,128]{1,0:T(8,128)(2,1)S(1)}, u32[]{:S(2)}, u32[]{:S(2)}) collective-permute-start(bf16[64,128]{1,0:T(8,128)(2,1)S(1)} %fusion.26), channel_id=1, source_target_pairs={{0,16},{16,32},{32,48},{48,64},{64,80},{80,96},{96,112},{112,128},... | collective-permute-start | bytes 49160 | tf_op jit(solution)/shard_map/ppermute | solution.py:61
  139.0 7.9 %collective-permute-start.6 = (bf16[64,128]{1,0:T(8,128)(2,1)S(1)}, bf16[64,128]{1,0:T(8,128)(2,1)S(1)}, u32[]{:S(2)}, u32[]{:S(2)}) collective-permute-start(bf16[64,128]{1,0:T(8,128)(2,1)S(1)} %fusion.25), channel_id=1, source_target_pairs={{0,16},{16,32},{32,48},{48,64},{64,80},{80,96},{96,112},{112,128},... | collective-permute-start | bytes 49160 | tf_op jit(solution)/shard_map/ppermute | solution.py:61
  147.6 7.7 %collective-permute-start.7 = (bf16[64,128]{1,0:T(8,128)(2,1)S(1)}, bf16[64,128]{1,0:T(8,128)(2,1)S(1)}, u32[]{:S(2)}, u32[]{:S(2)}) collective-permute-start(bf16[64,128]{1,0:T(8,128)(2,1)S(1)} %fusion.24), channel_id=1, source_target_pairs={{0,16},{16,32},{32,48},{48,64},{64,80},{80,96},{96,112},{112,128},... | collective-permute-start | bytes 49160 | tf_op jit(solution)/shard_map/ppermute | solution.py:61
  156.1 7.7 %collective-permute-start.8 = (bf16[64,128]{1,0:T(8,128)(2,1)S(1)}, bf16[64,128]{1,0:T(8,128)(2,1)S(1)}, u32[]{:S(2)}, u32[]{:S(2)}) collective-permute-start(bf16[64,128]{1,0:T(8,128)(2,1)S(1)} %fusion.23), channel_id=1, source_target_pairs={{0,16},{16,32},{32,48},{48,64},{64,80},{80,96},{96,112},{112,128},... | collective-permute-start | bytes 49160 | tf_op jit(solution)/shard_map/ppermute | solution.py:61
  164.6 7.7 %collective-permute-start.9 = (bf16[64,128]{1,0:T(8,128)(2,1)S(1)}, bf16[64,128]{1,0:T(8,128)(2,1)S(1)}, u32[]{:S(2)}, u32[]{:S(2)}) collective-permute-start(bf16[64,128]{1,0:T(8,128)(2,1)S(1)} %fusion.22), channel_id=1, source_target_pairs={{0,16},{16,32},{32,48},{48,64},{64,80},{80,96},{96,112},{112,128},... | collective-permute-start | bytes 49160 | tf_op jit(solution)/shard_map/ppermute | solution.py:61
  173.1 7.7 %collective-permute-start.10 = (bf16[64,128]{1,0:T(8,128)(2,1)S(1)}, bf16[64,128]{1,0:T(8,128)(2,1)S(1)}, u32[]{:S(2)}, u32[]{:S(2)}) collective-permute-start(bf16[64,128]{1,0:T(8,128)(2,1)S(1)} %fusion.21), channel_id=1, source_target_pairs={{0,16},{16,32},{32,48},{48,64},{64,80},{80,96},{96,112},{112,128},... | collective-permute-start | bytes 49160 | tf_op jit(solution)/shard_map/ppermute | solution.py:61
  181.6 7.7 %collective-permute-start.11 = (bf16[64,128]{1,0:T(8,128)(2,1)S(1)}, bf16[64,128]{1,0:T(8,128)(2,1)S(1)}, u32[]{:S(2)}, u32[]{:S(2)}) collective-permute-start(bf16[64,128]{1,0:T(8,128)(2,1)S(1)} %fusion.20), channel_id=1, source_target_pairs={{0,16},{16,32},{32,48},{48,64},{64,80},{80,96},{96,112},{112,128},... | collective-permute-start | bytes 49160 | tf_op jit(solution)/shard_map/ppermute | solution.py:61
  190.1 7.7 %collective-permute-start.12 = (bf16[64,128]{1,0:T(8,128)(2,1)S(1)}, bf16[64,128]{1,0:T(8,128)(2,1)S(1)}, u32[]{:S(2)}, u32[]{:S(2)}) collective-permute-start(bf16[64,128]{1,0:T(8,128)(2,1)S(1)} %fusion.19), channel_id=1, source_target_pairs={{0,16},{16,32},{32,48},{48,64},{64,80},{80,96},{96,112},{112,128},... | collective-permute-start | bytes 49160 | tf_op jit(solution)/shard_map/ppermute | solution.py:61
  198.7 7.7 %collective-permute-start.13 = (bf16[64,128]{1,0:T(8,128)(2,1)S(1)}, bf16[64,128]{1,0:T(8,128)(2,1)S(1)}, u32[]{:S(2)}, u32[]{:S(2)}) collective-permute-start(bf16[64,128]{1,0:T(8,128)(2,1)S(1)} %fusion.18), channel_id=1, source_target_pairs={{0,16},{16,32},{32,48},{48,64},{64,80},{80,96},{96,112},{112,128},... | collective-permute-start | bytes 49160 | tf_op jit(solution)/shard_map/ppermute | solution.py:61
  207.2 7.7 %collective-permute-start.14 = (bf16[64,128]{1,0:T(8,128)(2,1)S(1)}, bf16[64,128]{1,0:T(8,128)(2,1)S(1)}, u32[]{:S(2)}, u32[]{:S(2)}) collective-permute-start(bf16[64,128]{1,0:T(8,128)(2,1)S(1)} %fusion.17), channel_id=1, source_target_pairs={{0,16},{16,32},{32,48},{48,64},{64,80},{80,96},{96,112},{112,128},... | collective-permute-start | bytes 49160 | tf_op jit(solution)/shard_map/ppermute | solution.py:61
  215.7 2.6 collective-permute-start.15
Sparse Core Ops, SparseCore 0:
  9.5 47.2 all-gather.6
